TPU v7x, 128 devices: a whole 4x4x4 slice. The times are simulated.
128 devices in a mesh: row: 4 (over z), col: 32 (over x, y, core).
Axes of the slice: x: 4, y: 4, z: 4, core: 2. Of those that a mesh axis runs over, the one named last changes fastest.
Arguments:
- matrix_real: bfloat16 [512, 16384], P('col', 'row'), may hold values from -0.25 to 0.25
- matrix_imag: bfloat16 [512, 16384], P('col', 'row'), may hold values from -0.25 to 0.25
- valence_index: int32 [512], P('col'), may hold values from 0 to 15
- conduction_index: int32 [512], P('col'), may hold values from 0 to 31
- valence_energy: float32 [16], replicated, may hold values from -1.5 to -0.1
- conduction_energy: float32 [32], replicated, may hold values from 0.1 to 2
- frequency: float32 [2], replicated, may hold values from 0.2 to 2
Outputs:
- chi_real: bfloat16 [2, 16384, 16384], P(None, 'row', 'col')
- chi_imag: bfloat16 [2, 16384, 16384], P(None, 'row', 'col')
All inputs are finite; a program needn't handle non-finite values.
Results may differ from a plain program's by a relative error of at most 0.005.
Values may be sent and summed in bfloat16 or wider, within the bound.
No kernel may reach another device: no remote copies, remote signals or barrier semaphores. Data moves between devices by JAX's collectives and lax.ppermute only.
A program may use at most 192 MiB of HBM per device.

v0:
```python
import jax
import jax.numpy as jnp
from jax import lax
from jax.sharding import PartitionSpec as P


def lookup(indices, table):
    count = table.shape[0]
    picks = indices[:, None] == lax.broadcasted_iota(jnp.int32, (1, count), 1)
    return jnp.sum(jnp.where(picks, table[None, :], 0.0), axis=1)


def contract(left_side, right_side):
    return lax.dot_general(
        left_side, right_side, (((0,), (0,)), ((), ())), preferred_element_type=jnp.float32
    )


CHUNKS = 4


def on_device(
    matrix_real,
    matrix_imag,
    valence_index,
    conduction_index,
    valence_energy,
    conduction_energy,
    frequency,
):
    ncol = lax.psum(1, "col")
    local_pairs, local_g = matrix_real.shape
    pairs = local_pairs * ncol
    both = jnp.stack([matrix_real, matrix_imag])
    bands = jnp.stack([valence_index, conduction_index]).astype(jnp.float32)
    all_bands = lax.all_gather(bands, "col", axis=1, tiled=True).astype(jnp.int32)
    gap = lookup(all_bands[1], conduction_energy) - lookup(all_bands[0], valence_energy)
    spread = lax.all_gather(both, "row", axis=2, tiled=True)
    spread = spread.reshape(2, local_pairs, ncol, -1)
    column = lax.all_to_all(spread, "col", split_axis=2, concat_axis=1, tiled=True)
    width = column.shape[-1]
    wide = column.reshape(2, pairs, width).astype(jnp.float32)
    right_real = []
    right_imag = []
    for index in range(frequency.shape[0]):
        omega = frequency[index]
        weight = 4.0 * gap / (gap * gap + omega * omega)
        scaled_real = (weight[:, None] * wide[0]).astype(jnp.bfloat16)
        scaled_imag = (weight[:, None] * wide[1]).astype(jnp.bfloat16)
        right_real.append(jnp.concatenate([-scaled_real, -scaled_imag], axis=0))
        right_imag.append(jnp.concatenate([-scaled_imag, scaled_real], axis=0))
    step = local_g // CHUNKS
    real_parts = [[] for _ in right_real]
    imag_parts = [[] for _ in right_real]
    for chunk in range(CHUNKS):
        piece = both[:, :, chunk * step : (chunk + 1) * step]
        left = lax.all_gather(piece, "col", axis=1, tiled=True).reshape(2 * pairs, step)
        for index in range(len(right_real)):
            real_parts[index].append(contract(left, right_real[index]).astype(jnp.bfloat16))
            imag_parts[index].append(contract(left, right_imag[index]).astype(jnp.bfloat16))
    chi_real = jnp.stack([jnp.concatenate(p, axis=0) for p in real_parts])
    chi_imag = jnp.stack([jnp.concatenate(p, axis=0) for p in imag_parts])
    return (chi_real, chi_imag)


def solution(mesh):
    placed = (P("col", "row"), P("col", "row"), P("col"), P("col"), P(), P(), P())
    return jax.shard_map(
        on_device,
        mesh=mesh,
        in_specs=placed,
        out_specs=(P(None, "row", "col"), P(None, "row", "col")),
        check_vma=False,
    )
```

profile of v0, /device:TPU:1, one launch (start us, length us, event | category | flops | bytes accessed | tf_op | source)
XLA Modules:
  0.0 271.8 jit_solution(17406845412309366294)
XLA Ops:
  7.2 1.7 pad_maximum_fusion.6
  11.9 24.9 %all-gather.9.cloned.1.call-done = bf16[2,16,16384]{2,1,0:T(8,128)(2,1)} async-done(((bf16[2,16,4096]{2,1,0:T(8,128)(2,1)}), bf16[2,16,16384]{2,1,0:T(8,128)(2,1)}) %all-gather.9.cloned.1.call-update) | async-done | bytes 1048592 | tf_op jit(solution)/shard_map/all_gather | solution.py:38
  36.8 2.4 copy.26
  39.2 8.4 %all-to-all-start = ((bf16[2,16,32,512]{3,1,0,2:T(8,128)(2,1)}), bf16[2,16,32,512]{3,1,0,2:T(8,128)(2,1)S(1)}, u32[]{:S(2)}, u32[]{:S(2)}) async-start(bf16[2,16,32,512]{3,1,0,2:T(8,128)(2,1)} %bitcast.71), calls=%async_computation | async-start | bytes 2097152 | tf_op jit(solution)/shard_map/all_to_all | solution.py:40
  51.3 29.0 %all-gather = f32[32,16,2]{1,2,0:T(2,128)S(1)} all-gather(f32[1,16,2]{1,2,0:T(2,128)S(1)} %fusion.10), channel_id=1, replica_groups=mesh['row'=4,'col'=32] {'col'}, dimensions={0}, use_global_device_ids=true | all-gather | bytes 4224 | tf_op jit(solution)/shard_map/all_gather | solution.py:36
  82.7 5.7 %all-gather.11.cloned.1.call-done = bf16[2,512,1024]{2,1,0:T(8,128)(2,1)} async-done(((bf16[2,16,1024]{2,1,0:T(8,128)(2,1)}), bf16[2,512,1024]{2,1,0:T(8,128)(2,1)}) %all-gather.11.cloned.1.call-update) | async-done | bytes 2097168 | tf_op jit(solution)/shard_map/all_gather | solution.py:57
  88.4 3.8 %convolution_convert_fusion.10 = bf16[1024,512]{1,0:T(8,128)(2,1)} fusion(bf16[1024,1024]{1,0:T(8,128)(2,1)} %bitcast.82, bf16[512,512]{1,0:T(8,128)(2,1)S(1)} %get-tuple-element.11, bf16[512,512]{1,0:T(8,128)(2,1)S(1)} %get-tuple-element.16), kind=kOutput, calls=%fused_computation.17 | convolution fusion | flops 1076363264 | bytes 4194304 | tf_op jit(solution)/shard_map/dot_general | solution.py:14
  92.3 41.5 %all-gather.7.cloned.1.call-done = bf16[2,512,1024]{2,1,0:T(8,128)(2,1)} async-done(((bf16[2,16,1024]{2,1,0:T(8,128)(2,1)}), bf16[2,512,1024]{2,1,0:T(8,128)(2,1)}) %all-gather.7.cloned.1.call-update) | async-done | bytes 2097168 | tf_op jit(solution)/shard_map/all_gather | solution.py:57
  133.8 4.0 %convolution_convert_fusion.11 = bf16[1024,512]{1,0:T(8,128)(2,1)} fusion(bf16[1024,1024]{1,0:T(8,128)(2,1)} %bitcast.86, bf16[512,512]{1,0:T(8,128)(2,1)S(1)} %get-tuple-element.11, bf16[512,512]{1,0:T(8,128)(2,1)S(1)} %get-tuple-element.16), kind=kOutput, calls=%fused_computation.18 | convolution fusion | flops 1076363264 | bytes 4194304 | tf_op jit(solution)/shard_map/dot_general | solution.py:14
  139.3 2.5 convolution_convert_fusion.2
  141.9 37.1 %all-gather.13.cloned.1.call-done = bf16[2,512,1024]{2,1,0:T(8,128)(2,1)} async-done(((bf16[2,16,1024]{2,1,0:T(8,128)(2,1)}), bf16[2,512,1024]{2,1,0:T(8,128)(2,1)}) %all-gather.13.cloned.1.call-update) | async-done | bytes 2097168 | tf_op jit(solution)/shard_map/all_gather | solution.py:57
  179.0 4.2 %convolution_convert_fusion.9 = bf16[1024,512]{1,0:T(8,128)(2,1)} fusion(bf16[1024,1024]{1,0:T(8,128)(2,1)} %bitcast.90, bf16[512,512]{1,0:T(8,128)(2,1)} %copy-done.5, bf16[512,512]{1,0:T(8,128)(2,1)} %copy-done.11), kind=kOutput, calls=%fused_computation.16 | convolution fusion | flops 1076363264 | bytes 4194304 | tf_op jit(solution)/shard_map/dot_general | solution.py:14
  183.2 2.3 convolution_convert_fusion.1
  185.5 38.7 %all-gather.15.cloned.1.call-done = bf16[2,512,1024]{2,1,0:T(8,128)(2,1)} async-done(((bf16[2,16,1024]{2,1,0:T(8,128)(2,1)}), bf16[2,512,1024]{2,1,0:T(8,128)(2,1)}) %all-gather.15.cloned.1.call-update) | async-done | bytes 2097168 | tf_op jit(solution)/shard_map/all_gather | solution.py:57
  224.2 3.3 %convolution_convert_fusion.8 = bf16[1024,512]{1,0:T(8,128)(2,1)S(1)} fusion(bf16[1024,1024]{1,0:T(8,128)(2,1)} %bitcast.94, bf16[512,512]{1,0:T(8,128)(2,1)} %copy-done.5, bf16[512,512]{1,0:T(8,128)(2,1)} %copy-done.11), kind=kOutput, calls=%fused_computation.15 | convolution fusion | flops 1076363264 | bytes 4194304 | tf_op jit(solution)/shard_map/dot_general | solution.py:14
  227.5 2.3 convolution_convert_fusion
  232.7 2.5 convolution_convert_fusion.6
  235.2 2.3 convolution_convert_fusion.5
  238.8 2.4 convolution_convert_fusion.4
  241.2 2.3 convolution_convert_fusion.7
  245.3 2.8 %maximum_bitcast_fusion = (bf16[1,4096,512]{2,1,0:T(8,128)(2,1)S(1)}, bf16[1,4096,512]{2,1,0:T(8,128)(2,1)}) fusion(bf16[1024,512]{1,0:T(8,128)(2,1)S(1)} %convolution_convert_fusion.12, bf16[1024,512]{1,0:T(8,128)(2,1)S(1)} %convolution_convert_fusion.13, bf16[1024,512]{1,0:T(8,128)(2,1)S(1)} %convolution_convert_fusion.14, ...), kind=kLoop, calls=%fused_computation.2 | loop fusion | flops 33554432 | bytes 16777216 | tf_op jit(solution)/shard_map/stack | solution.py:61
  248.1 6.3 %pad_maximum_fusion = bf16[2,4096,512]{2,1,0:T(8,128)(2,1)} fusion(bf16[1,4096,512]{2,1,0:T(8,128)(2,1)} %get-tuple-element.27, bf16[1,4096,512]{2,1,0:T(8,128)(2,1)S(1)} %get-tuple-element.26), kind=kLoop, calls=%fused_computation | loop fusion | flops 4194304 | bytes 16777216 | tf_op jit(solution)/shard_map/stack | solution.py:61
  254.5 4.4 %maximum_bitcast_fusion.2 = (bf16[1,4096,512]{2,1,0:T(8,128)(2,1)S(1)}, bf16[1,4096,512]{2,1,0:T(8,128)(2,1)}) fusion(bf16[1024,512]{1,0:T(8,128)(2,1)} %convolution_convert_fusion.4, bf16[1024,512]{1,0:T(8,128)(2,1)} %convolution_convert_fusion.5, bf16[1024,512]{1,0:T(8,128)(2,1)} %convolution_convert_fusion.6, ...), kind=kLoop, calls=%fused_computation.4 | loop fusion | flops 33554432 | bytes 16777216 | tf_op jit(solution)/shard_map/stack | solution.py:62
  258.9 6.3 %pad_maximum_fusion.1 = bf16[2,4096,512]{2,1,0:T(8,128)(2,1)} fusion(bf16[1,4096,512]{2,1,0:T(8,128)(2,1)} %get-tuple-element.29, bf16[1,4096,512]{2,1,0:T(8,128)(2,1)S(1)} %get-tuple-element.28), kind=kLoop, calls=%fused_computation.1 | loop fusion | flops 4194304 | bytes 16777216 | tf_op jit(solution)/shard_map/stack | solution.py:62
  (78 shorter events, 14.1 us)
Async XLA Ops:
  7.2 29.6 %all-gather.9.cloned.1.call-start = ((), (), s32[]{:S(2)}) async-start(), calls=%async_computation.2 | async-start | bytes 1310720 | tf_op jit(solution)/shard_map/all_gather | solution.py:38
  8.9 79.5 %all-gather.11.cloned.1.call-start = ((), (), s32[]{:S(2)}) async-start(), calls=%async_computation.3 | async-start | bytes 2162688 | tf_op jit(solution)/shard_map/all_gather | solution.py:57
  10.6 123.2 %all-gather.7.cloned.1.call-start = ((), (), s32[]{:S(2)}) async-start(), calls=%async_computation.1 | async-start | bytes 2162688 | tf_op jit(solution)/shard_map/all_gather | solution.py:57
  11.3 167.7 %all-gather.13.cloned.1.call-start = ((), (), s32[]{:S(2)}) async-start(), calls=%async_computation.4 | async-start | bytes 2162688 | tf_op jit(solution)/shard_map/all_gather | solution.py:57
  36.8 11.5 %copy-start.12 = (f32[2]{0:T(128)S(1)}, f32[2]{0:T(128)}, u32[]{:S(2)}) copy-start(f32[2]{0:T(128)} %param.13) | copy-start | bytes 28
  36.8 14.5 %copy-start.15 = (s32[16]{0:T(128)S(1)}, s32[16]{0:T(128)}, u32[]{:S(2)}) copy-start(s32[16]{0:T(128)} %param.10) | copy-start | bytes 196
  36.8 14.5 %copy-start.16 = (s32[16]{0:T(128)S(1)}, s32[16]{0:T(128)}, u32[]{:S(2)}) copy-start(s32[16]{0:T(128)} %param.9) | copy-start | bytes 196
  36.8 43.8 %copy-start.13 = (f32[16]{0:T(128)S(1)}, f32[16]{0:T(128)}, u32[]{:S(2)}) copy-start(f32[16]{0:T(128)} %param.11) | copy-start | bytes 196
  36.8 43.9 %copy-start.14 = (f32[32]{0:T(128)S(1)}, f32[32]{0:T(128)}, u32[]{:S(2)}) copy-start(f32[32]{0:T(128)} %param.12) | copy-start | bytes 388
  39.2 41.6 %all-to-all-start = ((bf16[2,16,32,512]{3,1,0,2:T(8,128)(2,1)}), bf16[2,16,32,512]{3,1,0,2:T(8,128)(2,1)S(1)}, u32[]{:S(2)}, u32[]{:S(2)}) async-start(bf16[2,16,32,512]{3,1,0,2:T(8,128)(2,1)} %bitcast.71), calls=%async_computation | async-start | bytes 2097152 | tf_op jit(solution)/shard_map/all_to_all | solution.py:40
  47.6 176.6 %all-gather.15.cloned.1.call-start = ((), (), s32[]{:S(2)}) async-start(), calls=%async_computation.5 | async-start | bytes 2162688 | tf_op jit(solution)/shard_map/all_gather | solution.py:57
  82.7 51.0 %copy-start.11 = (bf16[512,512]{1,0:T(8,128)(2,1)}, bf16[512,512]{1,0:T(8,128)(2,1)S(1)}, u32[]{:S(2)}) copy-start(bf16[512,512]{1,0:T(8,128)(2,1)S(1)} %get-tuple-element.16) | copy-start | bytes 1572868
  82.7 55.0 %copy-start.5 = (bf16[512,512]{1,0:T(8,128)(2,1)}, bf16[512,512]{1,0:T(8,128)(2,1)S(1)}, u32[]{:S(2)}) copy-start(bf16[512,512]{1,0:T(8,128)(2,1)S(1)} %get-tuple-element.11) | copy-start | bytes 1572868
  82.7 55.0 %copy-start.8 = (bf16[512,512]{1,0:T(8,128)(2,1)}, bf16[512,512]{1,0:T(8,128)(2,1)S(1)}, u32[]{:S(2)}) copy-start(bf16[512,512]{1,0:T(8,128)(2,1)S(1)} %get-tuple-element.17) | copy-start | bytes 1572868
  133.7 4.0 %copy-start.19 = (bf16[2,512,1024]{2,1,0:T(8,128)(2,1)S(1)}, bf16[2,512,1024]{2,1,0:T(8,128)(2,1)}, u32[]{:S(2)}) copy-start(bf16[2,512,1024]{2,1,0:T(8,128)(2,1)} %all-gather.7.cloned.1.call-done) | copy-start | bytes 6291460
  179.0 4.2 %copy-start.6 = (bf16[512,512]{1,0:T(8,128)(2,1)S(1)}, bf16[512,512]{1,0:T(8,128)(2,1)}, u32[]{:S(2)}) copy-start(bf16[512,512]{1,0:T(8,128)(2,1)} %copy-done.5) | copy-start | bytes 1572868
  179.0 4.2 %copy-start.9 = (bf16[512,512]{1,0:T(8,128)(2,1)S(1)}, bf16[512,512]{1,0:T(8,128)(2,1)}, u32[]{:S(2)}) copy-start(bf16[512,512]{1,0:T(8,128)(2,1)} %copy-done.8) | copy-start | bytes 1572868
  179.0 4.2 %copy-start.21 = (bf16[2,512,1024]{2,1,0:T(8,128)(2,1)S(1)}, bf16[2,512,1024]{2,1,0:T(8,128)(2,1)}, u32[]{:S(2)}) copy-start(bf16[2,512,1024]{2,1,0:T(8,128)(2,1)} %all-gather.13.cloned.1.call-done) | copy-start | bytes 6291460
  224.2 3.3 %copy-start.7 = (bf16[512,512]{1,0:T(8,128)(2,1)S(1)}, bf16[512,512]{1,0:T(8,128)(2,1)}, u32[]{:S(2)}) copy-start(bf16[512,512]{1,0:T(8,128)(2,1)} %copy-done.5) | copy-start | bytes 1572868
  224.2 3.3 %copy-start.10 = (bf16[512,512]{1,0:T(8,128)(2,1)S(1)}, bf16[512,512]{1,0:T(8,128)(2,1)}, u32[]{:S(2)}) copy-start(bf16[512,512]{1,0:T(8,128)(2,1)} %copy-done.8) | copy-start | bytes 1572868
  224.2 3.3 %copy-start.23 = (bf16[2,512,1024]{2,1,0:T(8,128)(2,1)S(1)}, bf16[2,512,1024]{2,1,0:T(8,128)(2,1)}, u32[]{:S(2)}) copy-start(bf16[2,512,1024]{2,1,0:T(8,128)(2,1)} %all-gather.15.cloned.1.call-done) | copy-start | bytes 6291460
  227.5 2.3 copy-start.3
  227.5 2.3 copy-start.18
  238.8 2.4 copy-start.20
  (6 other events, 9.2 us)
Sparse Core Ops, SparseCore 0:
  10.2 26.4 all-gather.8
  39.7 48.6 all-gather.10
  90.8 42.9 all-gather.6
  136.0 42.9 all-gather.12
  181.2 42.9 all-gather.14
where the time goes:
time: 272 us
  waiting for transfers between devices  150 us (55%)
  matrix products  38.2 us (14%)
  blocking collectives  29 us (11%)
  other arithmetic  25.1 us (9%)
  between operations  16.5 us (6%)
  starting transfers between devices  8.64 us (3%)
  local copies, waits for them, and re-layouts  4.61 us (2%)
    all_gather x4, waiting for transfers between devices, on_device(): lax.all_gather(piece, 'col', axis=1, tiled=True).reshape(2 * pairs, step)  123 us
    dot_general x16, matrix products, contract(): lax.dot_general(left_side, right_side, (((0,), (0,)), ((), ())), preferre...  38.2 us
    all_gather x1, blocking collectives, on_device(): lax.all_gather(bands, 'col', axis=1, tiled=True).astype(jnp.int32)  29 us
    all_gather x1, waiting for transfers between devices, on_device(): spread = lax.all_gather(both, 'row', axis=2, tiled=True)  24.9 us
    another operation x2, other arithmetic, on_device(): chi_imag = jnp.stack([jnp.concatenate(p, axis=0) for p in imag_parts])  10.8 us
    another operation x2, other arithmetic, on_device(): chi_real = jnp.stack([jnp.concatenate(p, axis=0) for p in real_parts])  9.18 us
    all_to_all x1, starting transfers between devices, on_device(): lax.all_to_all(spread, 'col', split_axis=2, concat_axis=1, tiled=True)  8.44 us
  transfers between devices with their start and end apart: 6, of which 5 were waited for; matrix products, arithmetic and copies ran while one was open for 9% of the time, Pallas kernels for 0%

commit v1 on v0

--- a/solution.py
+++ b/solution.py
@@ -35,7 +35,12 @@
     bands = jnp.stack([valence_index, conduction_index]).astype(jnp.float32)
     all_bands = lax.all_gather(bands, "col", axis=1, tiled=True).astype(jnp.int32)
     gap = lookup(all_bands[1], conduction_energy) - lookup(all_bands[0], valence_energy)
-    spread = lax.all_gather(both, "row", axis=2, tiled=True)
+    ring = [both]
+    for hop in range(3):
+        ring.append(lax.ppermute(ring[-1], "row", [(dev, (dev + 1) % 4) for dev in range(4)]))
+    spread = jnp.roll(
+        jnp.concatenate(ring[::-1], axis=2), (lax.axis_index("row") + 1) * ring[0].shape[2], axis=2
+    )
     spread = spread.reshape(2, local_pairs, ncol, -1)
     column = lax.all_to_all(spread, "col", split_axis=2, concat_axis=1, tiled=True)
     width = column.shape[-1]

time: 272 us -> 250 us (0.919)
  waiting for transfers between devices: 150 us -> 124 us
  starting transfers between devices: 8.64 us -> 12.7 us
    all_gather x1 -> x0, waiting for transfers between devices: 24.9 us -> none  [on_device(): spread = lax.all_gather(both, 'row', axis=2, tiled=True)]
    all_gather x4, waiting for transfers between devices: 123 us -> 99.6 us  [on_device(): lax.all_gather(piece, 'col', axis=1, tiled=True).reshape(2 * pairs, step)]
    ppermute x0 -> x3, waiting for transfers between devices: none -> 22.9 us  [on_device(): lax.ppermute(ring[-1], 'row', [(dev, (dev + 1) % 4) for dev in range(4)])]
  transfers between devices with their start and end apart: 6 -> 8, of which waited for: 5 -> 6; matrix products, arithmetic and copies ran while one was open for 9% -> 10% of each run, Pallas kernels for 0% -> 0%
where the time goes in v1:
time: 250 us
  waiting for transfers between devices  124 us (50%)
  matrix products  38.8 us (16%)
  blocking collectives  30 us (12%)
  other arithmetic  24.5 us (10%)
  between operations  16.4 us (7%)
  starting transfers between devices  12.7 us (5%)
  local copies, waits for them, and re-layouts  3.55 us (1%)
    all_gather x4, waiting for transfers between devices, on_device(): lax.all_gather(piece, 'col', axis=1, tiled=True).reshape(2 * pairs, step)  99.6 us
    dot_general x16, matrix products, contract(): lax.dot_general(left_side, right_side, (((0,), (0,)), ((), ())), preferre...  38.8 us
    all_gather x1, blocking collectives, on_device(): lax.all_gather(bands, 'col', axis=1, tiled=True).astype(jnp.int32)  30 us
    ppermute x3, waiting for transfers between devices, on_device(): lax.ppermute(ring[-1], 'row', [(dev, (dev + 1) % 4) for dev in range(4)])  22.9 us
    another operation x2, other arithmetic, on_device(): chi_imag = jnp.stack([jnp.concatenate(p, axis=0) for p in imag_parts])  10.8 us
    all_to_all x1, starting transfers between devices, on_device(): lax.all_to_all(spread, 'col', split_axis=2, concat_axis=1, tiled=True)  10 us
    another operation x2, other arithmetic, on_device(): chi_real = jnp.stack([jnp.concatenate(p, axis=0) for p in real_parts])  9.18 us
  transfers between devices with their start and end apart: 8, of which 6 were waited for; matrix products, arithmetic and copies ran while one was open for 10% of the time, Pallas kernels for 0%

profile of v1, /device:TPU:1, one launch (start us, length us, event | category | flops | bytes accessed | tf_op | source)
XLA Modules:
  0.0 249.7 jit_solution(16800353719141102892)
XLA Ops:
  10.7 2.5 %collective-permute-start = (bf16[2,16,4096]{2,1,0:T(8,128)(2,1)S(1)}, bf16[2,16,4096]{2,1,0:T(8,128)(2,1)S(1)}, u32[]{:S(2)}, u32[]{:S(2)}) collective-permute-start(bf16[2,16,4096]{2,1,0:T(8,128)(2,1)S(1)} %pad_maximum_fusion.6), channel_id=1, source_target_pairs={{0,32},{32,64},{64,96},{96,0},{1,33},{33,65},{65,97},{97,1},{2,34}... | collective-permute-start | bytes 786440 | tf_op jit(solution)/shard_map/ppermute | solution.py:40
  13.2 8.2 %collective-permute-done = bf16[2,16,4096]{2,1,0:T(8,128)(2,1)S(1)} collective-permute-done((bf16[2,16,4096]{2,1,0:T(8,128)(2,1)S(1)}, bf16[2,16,4096]{2,1,0:T(8,128)(2,1)S(1)}, u32[]{:S(2)}, u32[]{:S(2)}) %collective-permute-start) | collective-permute-done | bytes 262176 | tf_op jit(solution)/shard_map/ppermute | solution.py:40
  21.4 7.8 %collective-permute-done.1 = bf16[2,16,4096]{2,1,0:T(8,128)(2,1)S(1)} collective-permute-done((bf16[2,16,4096]{2,1,0:T(8,128)(2,1)S(1)}, bf16[2,16,4096]{2,1,0:T(8,128)(2,1)S(1)}, u32[]{:S(2)}, u32[]{:S(2)}) %collective-permute-start.1) | collective-permute-done | bytes 262176 | tf_op jit(solution)/shard_map/ppermute | solution.py:40
  29.2 6.9 %collective-permute-done.2 = bf16[2,16,4096]{2,1,0:T(8,128)(2,1)S(1)} collective-permute-done((bf16[2,16,4096]{2,1,0:T(8,128)(2,1)S(1)}, bf16[2,16,4096]{2,1,0:T(8,128)(2,1)S(1)}, u32[]{:S(2)}, u32[]{:S(2)}) %collective-permute-start.2) | collective-permute-done | bytes 262176 | tf_op jit(solution)/shard_map/ppermute | solution.py:40
  37.7 10.0 %all-to-all-start = ((bf16[2,16,32,512]{3,1,0,2:T(8,128)(2,1)}), bf16[2,16,32,512]{3,1,0,2:T(8,128)(2,1)S(1)}, u32[]{:S(2)}, u32[]{:S(2)}) async-start(bf16[2,16,32,512]{3,1,0,2:T(8,128)(2,1)} %bitcast.71), calls=%async_computation | async-start | bytes 2097152 | tf_op jit(solution)/shard_map/all_to_all | solution.py:45
  51.1 30.0 %all-gather = f32[32,16,2]{1,2,0:T(2,128)S(1)} all-gather(f32[1,16,2]{1,2,0:T(2,128)S(1)} %fusion.10), channel_id=1, replica_groups=mesh['row'=4,'col'=32] {'col'}, dimensions={0}, use_global_device_ids=true | all-gather | bytes 4224 | tf_op jit(solution)/shard_map/all_gather | solution.py:36
  83.5 4.4 %convolution_convert_fusion.10 = bf16[1024,512]{1,0:T(8,128)(2,1)} fusion(bf16[1024,1024]{1,0:T(8,128)(2,1)} %bitcast.86, bf16[512,512]{1,0:T(8,128)(2,1)S(1)} %get-tuple-element.11, bf16[512,512]{1,0:T(8,128)(2,1)S(1)} %get-tuple-element.16), kind=kOutput, calls=%fused_computation.17 | convolution fusion | flops 1076363264 | bytes 4194304 | tf_op jit(solution)/shard_map/dot_general | solution.py:14
  87.9 23.6 %all-gather.6.cloned.1.call-done = bf16[2,512,1024]{2,1,0:T(8,128)(2,1)} async-done(((bf16[2,16,1024]{2,1,0:T(8,128)(2,1)}), bf16[2,512,1024]{2,1,0:T(8,128)(2,1)}) %all-gather.6.cloned.1.call-update) | async-done | bytes 2097168 | tf_op jit(solution)/shard_map/all_gather | solution.py:62
  111.5 4.0 %convolution_convert_fusion.11 = bf16[1024,512]{1,0:T(8,128)(2,1)} fusion(bf16[1024,1024]{1,0:T(8,128)(2,1)} %bitcast.90, bf16[512,512]{1,0:T(8,128)(2,1)S(1)} %get-tuple-element.11, bf16[512,512]{1,0:T(8,128)(2,1)S(1)} %get-tuple-element.16), kind=kOutput, calls=%fused_computation.18 | convolution fusion | flops 1076363264 | bytes 4194304 | tf_op jit(solution)/shard_map/dot_general | solution.py:14
  117.1 2.5 convolution_convert_fusion.2
  119.6 37.3 %all-gather.10.cloned.1.call-done = bf16[2,512,1024]{2,1,0:T(8,128)(2,1)} async-done(((bf16[2,16,1024]{2,1,0:T(8,128)(2,1)}), bf16[2,512,1024]{2,1,0:T(8,128)(2,1)}) %all-gather.10.cloned.1.call-update) | async-done | bytes 2097168 | tf_op jit(solution)/shard_map/all_gather | solution.py:62
  156.9 4.2 %convolution_convert_fusion.9 = bf16[1024,512]{1,0:T(8,128)(2,1)} fusion(bf16[1024,1024]{1,0:T(8,128)(2,1)} %bitcast.94, bf16[512,512]{1,0:T(8,128)(2,1)} %copy-done.7, bf16[512,512]{1,0:T(8,128)(2,1)} %copy-done.13), kind=kOutput, calls=%fused_computation.16 | convolution fusion | flops 1076363264 | bytes 4194304 | tf_op jit(solution)/shard_map/dot_general | solution.py:14
  161.1 2.3 convolution_convert_fusion.1
  163.4 38.7 %all-gather.12.cloned.1.call-done = bf16[2,512,1024]{2,1,0:T(8,128)(2,1)} async-done(((bf16[2,16,1024]{2,1,0:T(8,128)(2,1)}), bf16[2,512,1024]{2,1,0:T(8,128)(2,1)}) %all-gather.12.cloned.1.call-update) | async-done | bytes 2097168 | tf_op jit(solution)/shard_map/all_gather | solution.py:62
  202.1 3.3 %convolution_convert_fusion.8 = bf16[1024,512]{1,0:T(8,128)(2,1)S(1)} fusion(bf16[1024,1024]{1,0:T(8,128)(2,1)} %bitcast.98, bf16[512,512]{1,0:T(8,128)(2,1)} %copy-done.7, bf16[512,512]{1,0:T(8,128)(2,1)} %copy-done.13), kind=kOutput, calls=%fused_computation.15 | convolution fusion | flops 1076363264 | bytes 4194304 | tf_op jit(solution)/shard_map/dot_general | solution.py:14
  205.4 2.3 convolution_convert_fusion
  210.6 2.5 %convolution_convert_fusion.6 = bf16[1024,512]{1,0:T(8,128)(2,1)} fusion(bf16[1024,1024]{1,0:T(8,128)(2,1)S(1)} %bitcast.89, bf16[512,512]{1,0:T(8,128)(2,1)S(1)} %copy-done.6, bf16[512,512]{1,0:T(8,128)(2,1)S(1)} %get-tuple-element.10), kind=kOutput, calls=%fused_computation.13 | convolution fusion | flops 1076363264 | bytes 4194304 | tf_op jit(solution)/shard_map/dot_general | solution.py:14
  213.1 2.3 convolution_convert_fusion.5
  216.7 2.4 convolution_convert_fusion.4
  219.1 2.3 convolution_convert_fusion.7
  223.2 2.8 %maximum_bitcast_fusion = (bf16[1,4096,512]{2,1,0:T(8,128)(2,1)S(1)}, bf16[1,4096,512]{2,1,0:T(8,128)(2,1)}) fusion(bf16[1024,512]{1,0:T(8,128)(2,1)S(1)} %convolution_convert_fusion.12, bf16[1024,512]{1,0:T(8,128)(2,1)S(1)} %convolution_convert_fusion.13, bf16[1024,512]{1,0:T(8,128)(2,1)S(1)} %convolution_convert_fusion.14, ...), kind=kLoop, calls=%fused_computation.2 | loop fusion | flops 33554432 | bytes 16777216 | tf_op jit(solution)/shard_map/stack | solution.py:66
  226.0 6.3 %pad_maximum_fusion = bf16[2,4096,512]{2,1,0:T(8,128)(2,1)} fusion(bf16[1,4096,512]{2,1,0:T(8,128)(2,1)} %get-tuple-element.27, bf16[1,4096,512]{2,1,0:T(8,128)(2,1)S(1)} %get-tuple-element.26), kind=kLoop, calls=%fused_computation | loop fusion | flops 4194304 | bytes 16777216 | tf_op jit(solution)/shard_map/stack | solution.py:66
  232.4 4.4 %maximum_bitcast_fusion.2 = (bf16[1,4096,512]{2,1,0:T(8,128)(2,1)S(1)}, bf16[1,4096,512]{2,1,0:T(8,128)(2,1)}) fusion(bf16[1024,512]{1,0:T(8,128)(2,1)} %convolution_convert_fusion.4, bf16[1024,512]{1,0:T(8,128)(2,1)} %convolution_convert_fusion.5, bf16[1024,512]{1,0:T(8,128)(2,1)} %convolution_convert_fusion.6, ...), kind=kLoop, calls=%fused_computation.4 | loop fusion | flops 33554432 | bytes 16777216 | tf_op jit(solution)/shard_map/stack | solution.py:67
  236.8 6.3 %pad_maximum_fusion.1 = bf16[2,4096,512]{2,1,0:T(8,128)(2,1)} fusion(bf16[1,4096,512]{2,1,0:T(8,128)(2,1)} %get-tuple-element.29, bf16[1,4096,512]{2,1,0:T(8,128)(2,1)S(1)} %get-tuple-element.28), kind=kLoop, calls=%fused_computation.1 | loop fusion | flops 4194304 | bytes 16777216 | tf_op jit(solution)/shard_map/stack | solution.py:67
  (94 shorter events, 16.0 us)
Async XLA Ops:
  7.2 29.1 %copy-start.1 = (bf16[16,4096]{1,0:T(8,128)(2,1)S(1)}, bf16[16,4096]{1,0:T(8,128)(2,1)}, u32[]{:S(2)}) copy-start(bf16[16,4096]{1,0:T(8,128)(2,1)} %param.8) | copy-start | bytes 393220
  7.2 29.1 %copy-start = (bf16[16,4096]{1,0:T(8,128)(2,1)S(1)}, bf16[16,4096]{1,0:T(8,128)(2,1)}, u32[]{:S(2)}) copy-start(bf16[16,4096]{1,0:T(8,128)(2,1)} %param.7) | copy-start | bytes 393220
  7.2 76.3 %all-gather.8.cloned.1.call-start = ((), (), s32[]{:S(2)}) async-start(), calls=%async_computation.2 | async-start | bytes 2162688 | tf_op jit(solution)/shard_map/all_gather | solution.py:62
  8.9 102.6 %all-gather.6.cloned.1.call-start = ((), (), s32[]{:S(2)}) async-start(), calls=%async_computation.1 | async-start | bytes 2162688 | tf_op jit(solution)/shard_map/all_gather | solution.py:62
  9.6 147.2 %all-gather.10.cloned.1.call-start = ((), (), s32[]{:S(2)}) async-start(), calls=%async_computation.3 | async-start | bytes 2162688 | tf_op jit(solution)/shard_map/all_gather | solution.py:62
  10.7 10.7 %collective-permute-start = (bf16[2,16,4096]{2,1,0:T(8,128)(2,1)S(1)}, bf16[2,16,4096]{2,1,0:T(8,128)(2,1)S(1)}, u32[]{:S(2)}, u32[]{:S(2)}) collective-permute-start(bf16[2,16,4096]{2,1,0:T(8,128)(2,1)S(1)} %pad_maximum_fusion.6), channel_id=1, source_target_pairs={{0,32},{32,64},{64,96},{96,0},{1,33},{33,65},{65,97},{97,1},{2,34}... | collective-permute-start | bytes 786440 | tf_op jit(solution)/shard_map/ppermute | solution.py:40
  21.4 7.8 %collective-permute-start.1 = (bf16[2,16,4096]{2,1,0:T(8,128)(2,1)S(1)}, bf16[2,16,4096]{2,1,0:T(8,128)(2,1)S(1)}, u32[]{:S(2)}, u32[]{:S(2)}) collective-permute-start(bf16[2,16,4096]{2,1,0:T(8,128)(2,1)S(1)} %collective-permute-done), channel_id=1, source_target_pairs={{0,32},{32,64},{64,96},{96,0},{1,33},{33,65},{65,97},{97,1},{2,34}... | collective-permute-start | bytes 786440 | tf_op jit(solution)/shard_map/ppermute | solution.py:40
  29.2 7.0 %collective-permute-start.2 = (bf16[2,16,4096]{2,1,0:T(8,128)(2,1)S(1)}, bf16[2,16,4096]{2,1,0:T(8,128)(2,1)S(1)}, u32[]{:S(2)}, u32[]{:S(2)}) collective-permute-start(bf16[2,16,4096]{2,1,0:T(8,128)(2,1)S(1)} %collective-permute-done.1), channel_id=1, source_target_pairs={{0,32},{32,64},{64,96},{96,0},{1,33},{33,65},{65,97},{97,1},{2,34}... | collective-permute-start | bytes 786440 | tf_op jit(solution)/shard_map/ppermute | solution.py:40
  36.5 11.8 %copy-start.14 = (f32[2]{0:T(128)S(1)}, f32[2]{0:T(128)}, u32[]{:S(2)}) copy-start(f32[2]{0:T(128)} %param.13) | copy-start | bytes 28
  36.5 14.6 %copy-start.17 = (s32[16]{0:T(128)S(1)}, s32[16]{0:T(128)}, u32[]{:S(2)}) copy-start(s32[16]{0:T(128)} %param.10) | copy-start | bytes 196
  36.5 14.6 %copy-start.18 = (s32[16]{0:T(128)S(1)}, s32[16]{0:T(128)}, u32[]{:S(2)}) copy-start(s32[16]{0:T(128)} %param.9) | copy-start | bytes 196
  36.5 44.9 %copy-start.15 = (f32[16]{0:T(128)S(1)}, f32[16]{0:T(128)}, u32[]{:S(2)}) copy-start(f32[16]{0:T(128)} %param.11) | copy-start | bytes 196
  36.5 45.0 %copy-start.16 = (f32[32]{0:T(128)S(1)}, f32[32]{0:T(128)}, u32[]{:S(2)}) copy-start(f32[32]{0:T(128)} %param.12) | copy-start | bytes 388
  37.7 43.9 %all-to-all-start = ((bf16[2,16,32,512]{3,1,0,2:T(8,128)(2,1)}), bf16[2,16,32,512]{3,1,0,2:T(8,128)(2,1)S(1)}, u32[]{:S(2)}, u32[]{:S(2)}) async-start(bf16[2,16,32,512]{3,1,0,2:T(8,128)(2,1)} %bitcast.71), calls=%async_computation | async-start | bytes 2097152 | tf_op jit(solution)/shard_map/all_to_all | solution.py:45
  47.7 154.4 %all-gather.12.cloned.1.call-start = ((), (), s32[]{:S(2)}) async-start(), calls=%async_computation.4 | async-start | bytes 2162688 | tf_op jit(solution)/shard_map/all_gather | solution.py:62
  83.5 28.0 %copy-start.13 = (bf16[512,512]{1,0:T(8,128)(2,1)}, bf16[512,512]{1,0:T(8,128)(2,1)S(1)}, u32[]{:S(2)}) copy-start(bf16[512,512]{1,0:T(8,128)(2,1)S(1)} %get-tuple-element.16) | copy-start | bytes 1572868
  83.5 32.0 %copy-start.7 = (bf16[512,512]{1,0:T(8,128)(2,1)}, bf16[512,512]{1,0:T(8,128)(2,1)S(1)}, u32[]{:S(2)}) copy-start(bf16[512,512]{1,0:T(8,128)(2,1)S(1)} %get-tuple-element.11) | copy-start | bytes 1572868
  83.5 32.0 %copy-start.10 = (bf16[512,512]{1,0:T(8,128)(2,1)}, bf16[512,512]{1,0:T(8,128)(2,1)S(1)}, u32[]{:S(2)}) copy-start(bf16[512,512]{1,0:T(8,128)(2,1)S(1)} %get-tuple-element.17) | copy-start | bytes 1572868
  111.5 4.0 %copy-start.21 = (bf16[2,512,1024]{2,1,0:T(8,128)(2,1)S(1)}, bf16[2,512,1024]{2,1,0:T(8,128)(2,1)}, u32[]{:S(2)}) copy-start(bf16[2,512,1024]{2,1,0:T(8,128)(2,1)} %all-gather.6.cloned.1.call-done) | copy-start | bytes 6291460
  156.9 4.2 %copy-start.8 = (bf16[512,512]{1,0:T(8,128)(2,1)S(1)}, bf16[512,512]{1,0:T(8,128)(2,1)}, u32[]{:S(2)}) copy-start(bf16[512,512]{1,0:T(8,128)(2,1)} %copy-done.7) | copy-start | bytes 1572868
  156.9 4.2 %copy-start.11 = (bf16[512,512]{1,0:T(8,128)(2,1)S(1)}, bf16[512,512]{1,0:T(8,128)(2,1)}, u32[]{:S(2)}) copy-start(bf16[512,512]{1,0:T(8,128)(2,1)} %copy-done.10) | copy-start | bytes 1572868
  156.9 4.2 %copy-start.23 = (bf16[2,512,1024]{2,1,0:T(8,128)(2,1)S(1)}, bf16[2,512,1024]{2,1,0:T(8,128)(2,1)}, u32[]{:S(2)}) copy-start(bf16[2,512,1024]{2,1,0:T(8,128)(2,1)} %all-gather.10.cloned.1.call-done) | copy-start | bytes 6291460
  202.1 3.3 %copy-start.12 = (bf16[512,512]{1,0:T(8,128)(2,1)S(1)}, bf16[512,512]{1,0:T(8,128)(2,1)}, u32[]{:S(2)}) copy-start(bf16[512,512]{1,0:T(8,128)(2,1)} %copy-done.10) | copy-start | bytes 1572868
  202.1 3.3 %copy-start.25 = (bf16[2,512,1024]{2,1,0:T(8,128)(2,1)S(1)}, bf16[2,512,1024]{2,1,0:T(8,128)(2,1)}, u32[]{:S(2)}) copy-start(bf16[2,512,1024]{2,1,0:T(8,128)(2,1)} %all-gather.12.cloned.1.call-done) | copy-start | bytes 6291460
  (10 other events, 19.4 us)
Sparse Core Ops, SparseCore 0:
  11.0 52.8 all-gather.7
  66.3 45.1 all-gather.5
  113.9 42.9 all-gather.9
  159.1 42.9 all-gather.11
